TPU v7x, 128 devices: a whole 4x4x4 slice. The times are simulated.
128 devices in a mesh: tm: 16 (over z, x), space: 8 (over y, core).
Axes of the slice: x: 4, y: 4, z: 4, core: 2. Of those that a mesh axis runs over, the one named last changes fastest.
Arguments:
- query_states: bfloat16 [16, 2048, 2560], P('tm', 'space'), may hold values from -45 to 45
- key_states: bfloat16 [16, 2048, 2560], P('tm', 'space'), may hold values from -4 to 4
- value_states: bfloat16 [16, 2048, 2560], P('tm', 'space'), may hold values from -6 to 6
- history: int32 [16], P('tm'), may hold values from 0 to 2, as said below
- neighbours: int32 [16, 8, 2], P('tm', 'space'), may hold values 0 or 1
Outputs:
- attended: bfloat16 [16, 2048, 2560], P('tm', 'space')
Inputs may be any that keep to these rules, and one draw needn't show every extreme that they name: Some segment has history exactly 2 in every draw.
All inputs are finite; a program needn't handle non-finite values. No bound on the sum of `neighbours` on one device may be relied on, other than what follows from the above.
Results may differ from a plain program's by a relative error of at most 0.005.
Values may be sent and summed in bfloat16 or wider, within the bound.
No kernel may reach another device: no remote copies, remote signals or barrier semaphores. Data moves between devices by JAX's collectives and lax.ppermute only.
A program may use at most 128 MiB of HBM per device.

v0:
```python
import jax
import jax.numpy as jnp
from jax import lax
from jax.sharding import PartitionSpec as P

HEAD_DIM = 128
HIST_CH = 2


def extended_2(cells, sides, width):
    for axis, dim in sides:
        count = lax.axis_size(axis)
        ends = count - 1
        head = lax.slice_in_dim(cells, 0, width, axis=dim)
        tail = lax.slice_in_dim(cells, cells.shape[dim] - width, cells.shape[dim], axis=dim)
        cells = jnp.concatenate(
            [
                lax.ppermute(tail, axis, [(i, (i + 1) % count) for i in range(ends)]),
                cells,
                lax.ppermute(head, axis, [((i + 1) % count, i) for i in range(ends)]),
            ],
            axis=dim,
        )
    return cells


def passed_along(shard, axis, by):
    size = lax.axis_size(axis)
    pairs = [(i, i + by) for i in range(size) if 0 <= i + by < size]
    return lax.ppermute(shard, axis, pairs)


def absorb(state, kv_block, first_frame, query_rows, query_frame, window_start, side_flags):
    best, denom, accum = state
    tile_len = kv_block.shape[2] // 3
    row_count, head_count, head_dim = query_rows.shape
    inv_root = 1.0 / head_dim**0.5
    key_frame = first_frame + 0
    row_ok = (key_frame <= query_frame) & (key_frame >= window_start) & (key_frame >= 0)
    for third in range(3):
        lower = third * tile_len
        key_slab = kv_block[0, 0, lower : lower + tile_len].reshape(tile_len, head_count, head_dim)
        value_slab = kv_block[1, 0, lower : lower + tile_len].reshape(
            tile_len, head_count, head_dim
        )
        allowed = (row_ok & side_flags[third])[None, :, None]
        scores = (
            jnp.einsum("rhd,khd->hrk", query_rows, key_slab, preferred_element_type=jnp.float32)
            * inv_root
        )
        scores = jnp.where(allowed, scores, -1e30)
        newbest = jnp.maximum(best, jnp.max(scores, axis=-1))
        rescale = jnp.exp(best - newbest)
        weights = jnp.where(allowed, jnp.exp(scores - newbest[..., None]), 0.0)
        denom = denom * rescale + jnp.sum(weights, axis=-1)
        contrib = jnp.einsum(
            "hrk,khd->rhd",
            weights.astype(jnp.bfloat16),
            value_slab,
            preferred_element_type=jnp.float32,
        )
        accum = accum * jnp.transpose(rescale)[:, :, None] + contrib
        best = newbest
    return (best, denom, accum)


def on_device(query_states, key_states, value_states, history, neighbours):
    frames, tile_len, width_all = query_states.shape
    head_count = width_all // HEAD_DIM
    seg_index = lax.axis_index("tm")
    tile_index = lax.axis_index("space")
    tile_total = lax.axis_size("space")
    stacked = jnp.stack([key_states, value_states])
    blocks = []
    extended = extended_2(stacked, (("space", 2),), tile_len)
    blocks.append(extended)
    carried = extended
    for distance in range(1, HIST_CH + 1):
        carried = passed_along(carried, "tm", 1)
        blocks.append(carried)
    left_open = (neighbours[0, 0, 0] == 1) & (tile_index > 0)
    right_open = (neighbours[0, 0, 1] == 1) & (tile_index < tile_total - 1)
    side_flags = (left_open, jnp.array(True), right_open)
    query_rows = query_states.reshape(frames * tile_len, head_count, HEAD_DIM)
    query_frame = seg_index * frames + jnp.repeat(jnp.arange(frames, dtype=jnp.int32), tile_len)
    window_start = seg_index * frames - history[0]
    row_count = frames * tile_len
    state = (
        jnp.full((head_count, row_count), -1e30, jnp.float32),
        jnp.zeros((head_count, row_count), jnp.float32),
        jnp.zeros((row_count, head_count, HEAD_DIM), jnp.float32),
    )
    state = absorb(
        state, blocks[0], seg_index * frames, query_rows, query_frame, window_start, side_flags
    )
    for distance in range(1, HIST_CH + 1):
        kv_block = blocks[distance]
        first_frame = (seg_index - distance) * frames

        def take_block(current, kv_block=kv_block, first_frame=first_frame):
            return absorb(
                current, kv_block, first_frame, query_rows, query_frame, window_start, side_flags
            )

        state = take_block(state)
    best, denom, accum = state
    result = accum / jnp.transpose(denom)[:, :, None]
    return result.astype(jnp.bfloat16).reshape(frames, tile_len, width_all)


def solution(mesh):
    placed = (
        P("tm", "space", None),
        P("tm", "space", None),
        P("tm", "space", None),
        P("tm"),
        P("tm", "space", None),
    )
    return jax.shard_map(
        on_device, mesh=mesh, in_specs=placed, out_specs=P("tm", "space", None), check_vma=False
    )
```

profile of v0, /device:TPU:112, one launch (start us, length us, event | category | flops | bytes accessed | tf_op | source)
XLA Modules:
  0.0 453.2 jit_solution(1044365071108352488)
XLA Ops:
  3.5 2.1 collective-permute-start
  5.5 3.6 collective-permute-start.1
  9.2 27.4 %collective-permute-done = bf16[2,1,256,2560]{2,3,1,0:T(8,128)(2,1)S(1)} collective-permute-done((bf16[2,1,256,2560]{2,3,1,0:T(8,128)(2,1)S(1)}, bf16[2,1,256,2560]{2,3,1,0:T(8,128)(2,1)S(1)}, u32[]{:S(2)}, u32[]{:S(2)}) %collective-permute-start) | collective-permute-done | bytes 2621472 | tf_op jit(solution)/shard_map/ppermute | solution.py:18
  39.8 3.4 collective-permute-start.2
  43.2 172.3 %collective-permute-done.2 = bf16[2,1,768,2560]{2,3,1,0:T(8,128)(2,1)} collective-permute-done((bf16[2,1,768,2560]{2,3,1,0:T(8,128)(2,1)S(1)}, bf16[2,1,768,2560]{2,3,1,0:T(8,128)(2,1)}, u32[]{:S(2)}, u32[]{:S(2)}) %collective-permute-start.2) | collective-permute-done | bytes 7864352 | tf_op jit(solution)/shard_map/ppermute | solution.py:30
  226.5 3.3 bitcast_reduce_fusion.6
  229.8 5.3 %fusion.162 = (bf16[1,1,256,2560]{2,3,1,0:T(8,128)(2,1)}, bf16[1,1,256,2560]{2,3,1,0:T(8,128)(2,1)}, bf16[1,1,256,2560]{2,3,1,0:T(8,128)(2,1)S(1)}, bf16[1,1,256...) fusion(bf16[2,1,768,2560]{2,3,1,0:T(8,128)(2,1)} %collective-permute-done.2), kind=kLoop, calls=%fused_computation.212 | loop fusion | bytes 15728640 | tf_op jit(solution)/shard_map/slice | solution.py:43
  236.2 3.3 bitcast_reduce_fusion.5
  240.5 150.7 %collective-permute-done.3 = bf16[2,1,768,2560]{2,3,1,0:T(8,128)(2,1)} collective-permute-done((bf16[2,1,768,2560]{2,3,1,0:T(8,128)(2,1)}, bf16[2,1,768,2560]{2,3,1,0:T(8,128)(2,1)}, u32[]{:S(2)}, u32[]{:S(2)}) %collective-permute-start.3) | collective-permute-done | bytes 7864352 | tf_op jit(solution)/shard_map/ppermute | solution.py:30
  391.3 5.4 %fusion.161 = (bf16[1,1,256,2560]{2,3,1,0:T(8,128)(2,1)}, bf16[1,1,256,2560]{2,3,1,0:T(8,128)(2,1)S(1)}, bf16[1,1,256,2560]{2,3,1,0:T(8,128)(2,1)}, bf16[1,1,256...) fusion(bf16[2,1,768,2560]{2,3,1,0:T(8,128)(2,1)} %collective-permute-done.3), kind=kLoop, calls=%fused_computation.211 | loop fusion | bytes 15728640 | tf_op jit(solution)/shard_map/slice | solution.py:43
  398.7 3.3 bitcast_reduce_fusion.2
  402.1 2.8 fusion.49
  404.9 4.4 fusion.19
  409.3 5.2 %fusion.47 = f32[20,128,256]{2,1,0:T(8,128)} fusion(bf16[256,20,128]{0,2,1:T(8,128)(2,1)S(1)} %bitcast.371, f32[20,256,256]{2,1,0:T(8,128)} %get-tuple-element.57, f32[20,256]{1,0:T(8,128)S(1)} %get-tuple-element.21, pred[]{:T(512)S(6)} %and.70), kind=kOutput, calls=%fused_computation.68 | convolution fusion | flops 342097920 | bytes 9195521 | tf_op jit(solution)/shard_map/hrk,khd->rhd/dot_general | solution.py:56
  416.4 2.6 fusion.51
  419.0 5.4 %fusion.45 = f32[20,128,256]{2,1,0:T(8,128)} fusion(bf16[256,20,128]{0,2,1:T(8,128)(2,1)S(1)} %bitcast.378, f32[20,256,256]{2,1,0:T(8,128)} %get-tuple-element.55, f32[20,256]{1,0:T(8,128)S(1)} %get-tuple-element.20, pred[]{:T(512)S(6)} %and.73), kind=kOutput, calls=%fused_computation.67 | convolution fusion | flops 342097920 | bytes 9195521 | tf_op jit(solution)/shard_map/hrk,khd->rhd/dot_general | solution.py:56
  424.4 2.9 fusion.23
  427.3 2.7 fusion.43
  430.0 2.7 fusion.41
  433.3 2.7 fusion.27
  436.0 2.7 fusion.39
  438.7 2.7 fusion.37
  441.5 2.7 fusion.31
  445.2 6.4 %fusion.55 = bf16[256,20,128]{0,2,1:T(8,128)(2,1)S(1)} fusion(f32[20,128,256]{2,1,0:T(8,128)} %fusion.37, f32[20,128,256]{2,1,0:T(8,128)} %fusion.39, f32[20,128,256]{2,1,0:T(8,128)} %fusion.41, f32[20,128,256]{2,1,0:T(8,128)} %fusion.43, f32[20,128,256]{2,1,0:T(8,128)} %fusion.45, f32[20,128,256]{2,1,0:T(8,128)S(1)} %copy-done.15, ...), kind=kOutput, calls=%fused_computation.75 | convolution fusion | flops 354549760 | bytes 29061120 | tf_op jit(solution)/shard_map/hrk,khd->rhd/dot_general | solution.py:56
  (65 shorter events, 24.9 us)
Async XLA Ops:
  3.2 35.1 %copy-start = (bf16[1,256,2560]{1,2,0:T(8,128)(2,1)}, bf16[1,256,2560]{1,2,0:T(8,128)(2,1)S(1)}, u32[]{:S(2)}) copy-start(bf16[1,256,2560]{1,2,0:T(8,128)(2,1)S(1)} %copy.45) | copy-start | bytes 3932164
  3.5 214.6 %copy-start.13 = (s32[1,1,2]{2,1,0:T(1,128)S(1)}, s32[1,1,2]{2,1,0:T(1,128)}, u32[]{:S(2)}) copy-start(s32[1,1,2]{2,1,0:T(1,128)} %param.9) | copy-start | bytes 28
  3.5 33.1 %collective-permute-start = (bf16[2,1,256,2560]{2,3,1,0:T(8,128)(2,1)S(1)}, bf16[2,1,256,2560]{2,3,1,0:T(8,128)(2,1)S(1)}, u32[]{:S(2)}, u32[]{:S(2)}) collective-permute-start(bf16[2,1,256,2560]{2,3,1,0:T(8,128)(2,1)S(1)} %pad_maximum_fusion.1), channel_id=1, source_target_pairs={{0,1},{1,2},{2,3},{3,4},{4,5},{5,6},{6,7},{8,9},{9,10},{10,11},{11... | collective-permute-start | bytes 7864328 | tf_op jit(solution)/shard_map/ppermute | solution.py:18
  5.5 32.8 %collective-permute-start.1 = (bf16[2,1,256,2560]{2,3,1,0:T(8,128)(2,1)S(1)}, bf16[2,1,256,2560]{2,3,1,0:T(8,128)(2,1)S(1)}, u32[]{:S(2)}, u32[]{:S(2)}) collective-permute-start(bf16[2,1,256,2560]{2,3,1,0:T(8,128)(2,1)S(1)} %pad_maximum_fusion.1), channel_id=1, source_target_pairs={{1,0},{2,1},{3,2},{4,3},{5,4},{6,5},{7,6},{9,8},{10,9},{11,10},{12... | collective-permute-start | bytes 7864328 | tf_op jit(solution)/shard_map/ppermute | solution.py:20
  36.6 2.3 copy-start.4
  39.8 175.7 %collective-permute-start.2 = (bf16[2,1,768,2560]{2,3,1,0:T(8,128)(2,1)S(1)}, bf16[2,1,768,2560]{2,3,1,0:T(8,128)(2,1)}, u32[]{:S(2)}, u32[]{:S(2)}) collective-permute-start(bf16[2,1,768,2560]{2,3,1,0:T(8,128)(2,1)S(1)} %pad_maximum_fusion), channel_id=1, source_target_pairs={{0,8},{8,16},{16,24},{24,32},{32,40},{40,48},{48,56},{56,64},{64,7... | collective-permute-start | bytes 23592968 | tf_op jit(solution)/shard_map/ppermute | solution.py:30
  215.5 175.8 %collective-permute-start.3 = (bf16[2,1,768,2560]{2,3,1,0:T(8,128)(2,1)}, bf16[2,1,768,2560]{2,3,1,0:T(8,128)(2,1)}, u32[]{:S(2)}, u32[]{:S(2)}) collective-permute-start(bf16[2,1,768,2560]{2,3,1,0:T(8,128)(2,1)} %collective-permute-done.2), channel_id=1, source_target_pairs={{0,8},{8,16},{16,24},{24,32},{32,40},{40,48},{48,56},{56,64},{64,7... | collective-permute-start | bytes 23592968 | tf_op jit(solution)/shard_map/ppermute | solution.py:30
  221.6 1.7 copy-start.5
  224.6 1.7 copy-start.3
  398.7 3.4 copy-start.6
  414.5 1.9 copy-start.1
  416.4 2.6 copy-start.11
  419.0 5.4 %slice-start = ((s8[5242880]{0:T(1024)(128)(4,1)}), s8[4194304]{0:T(1024)(128)(4,1)S(1)}, s32[]{:S(2)}) async-start(s8[5242880]{0:T(1024)(128)(4,1)} %bitcast.353), calls=%async_computation | async-start | bytes 8388608
  419.0 5.4 %slice-start.1 = ((s8[5242880]{0:T(1024)(128)(4,1)}), s8[1048576]{0:T(1024)(128)(4,1)S(1)}, s32[]{:S(2)}) async-start(s8[5242880]{0:T(1024)(128)(4,1)} %bitcast.353), calls=%async_computation.1 | async-start | bytes 2097152
  424.4 2.9 copy-start.9
  427.3 2.7 copy-start.8
  430.0 2.7 slice-start.2
  430.0 3.3 slice-start.3
  433.3 2.7 copy-start.12
  436.0 2.7 copy-start.10
  441.5 2.8 copy-start.7
  441.5 2.8 copy-start.14
  441.5 2.9 copy-start.15
  441.5 3.7 copy-start.16
  (1 other events, 1.5 us)
where the time goes:
time: 454 us; the launch traced here: 453 us
  waiting for transfers between devices  352 us (78%)
  matrix products  49.9 us (11%)
  local copies, waits for them, and re-layouts  22.4 us (5%)
  other arithmetic  15.4 us (3%)
  starting transfers between devices  11 us (2%)
    ppermute x2, waiting for transfers between devices, passed_along(): return lax.ppermute(shard, axis, pairs)  323 us
    dot_general x9, matrix products, absorb(): jnp.einsum('hrk,khd->rhd', weights.astype(jnp.bfloat16), value_slab, pref...  33.3 us
    ppermute x1, waiting for transfers between devices, extended_2(): lax.ppermute(tail, axis, [(i, (i + 1) % count) for i in range(ends)])  27.4 us
    dot_general x9, matrix products, absorb(): jnp.einsum('rhd,khd->hrk', query_rows, key_slab, preferred_element_type=j...  16.6 us
    reduce_sum x5, other arithmetic, absorb(): denom = denom * rescale + jnp.sum(weights, axis=-1)  14.5 us
    slice x4, local copies, waits for them, and re-layouts, absorb(): kv_block[1, 0, lower:lower + tile_len]  12.1 us
  transfers between devices with their start and end apart: 4, of which 4 were waited for; matrix products, arithmetic and copies ran while one was open for 4% of the time, Pallas kernels for 0%

commit v1 on v0

v1 whole, which is shorter than its diff:
```python
import jax
import jax.numpy as jnp
from jax import lax
from jax.experimental import pallas as pl
from jax.experimental.pallas import tpu as pltpu
from jax.sharding import PartitionSpec as P

HEAD_DIM = 128
HIST_MAX = 2
HG = 5
CHUNKS = 1
NEG = -1e30


def _attn_kernel(flags_ref, q_ref, kl_ref, kc_ref, kr_ref, vl_ref, vc_ref, vr_ref, o_ref, lse_ref, col_ref):
    hg = q_ref.shape[1] // HEAD_DIM
    inv_root = 1.0 / HEAD_DIM**0.5
    seg_ok = flags_ref[1] == 1

    @pl.when(seg_ok)
    def _():
        bias_l = jnp.where(flags_ref[0] == 1, 0.0, NEG).astype(jnp.float32)
        bias_r = jnp.where(flags_ref[2] == 1, 0.0, NEG).astype(jnp.float32)
        col_ref[...] = jnp.zeros_like(col_ref)
        for h in range(hg):
            cols = slice(h * HEAD_DIM, (h + 1) * HEAD_DIM)
            q = q_ref[:, cols]

            def scores(k_ref):
                return (
                    lax.dot_general(
                        q, k_ref[:, cols], (((1,), (1,)), ((), ())), preferred_element_type=jnp.float32
                    )
                    * inv_root
                )

            s_l = scores(kl_ref) + bias_l
            s_c = scores(kc_ref)
            s_r = scores(kr_ref) + bias_r
            m = jnp.maximum(
                jnp.maximum(s_l.max(axis=1, keepdims=True), s_c.max(axis=1, keepdims=True)),
                s_r.max(axis=1, keepdims=True),
            )
            p_l = jnp.exp(s_l - m)
            p_c = jnp.exp(s_c - m)
            p_r = jnp.exp(s_r - m)
            denom = (
                p_l.sum(axis=1, keepdims=True) + p_c.sum(axis=1, keepdims=True) + p_r.sum(axis=1, keepdims=True)
            )
            acc = jnp.dot(p_l.astype(jnp.bfloat16), vl_ref[:, cols], preferred_element_type=jnp.float32)
            acc += jnp.dot(p_c.astype(jnp.bfloat16), vc_ref[:, cols], preferred_element_type=jnp.float32)
            acc += jnp.dot(p_r.astype(jnp.bfloat16), vr_ref[:, cols], preferred_element_type=jnp.float32)
            o_ref[:, cols] = (acc / denom).astype(o_ref.dtype)
            col_ref[:, h : h + 1] = m + jnp.log(denom)
        lse_ref[0] = jnp.transpose(col_ref[...])[:hg, :]

    @pl.when(jnp.logical_not(seg_ok))
    def _():
        o_ref[...] = jnp.zeros_like(o_ref)
        lse_ref[...] = jnp.full(lse_ref.shape, NEG, jnp.float32)


def attend(flags, q, keys, values, width, base, q_offset):
    rows = q.shape[0]
    heads = width // HEAD_DIM
    groups = heads // HG
    lanes = HG * HEAD_DIM
    q_spec = pl.BlockSpec((rows, lanes), lambda g, f: (0, g + q_offset))
    kv_spec = pl.BlockSpec((rows, lanes), lambda g, f: (0, g + base))
    keys_rows = keys[0].shape[0]
    flops = 4 * rows * 3 * keys_rows * HEAD_DIM * heads
    return pl.pallas_call(
        _attn_kernel,
        out_shape=(
            jax.ShapeDtypeStruct((rows, width), jnp.bfloat16),
            jax.ShapeDtypeStruct((groups, HG, rows), jnp.float32),
        ),
        grid_spec=pltpu.PrefetchScalarGridSpec(
            num_scalar_prefetch=1,
            grid=(groups,),
            in_specs=[q_spec] + [kv_spec] * 6,
            out_specs=[
                pl.BlockSpec((rows, lanes), lambda g, f: (0, g)),
                pl.BlockSpec((1, HG, rows), lambda g, f: (g, 0, 0)),
            ],
            scratch_shapes=[pltpu.VMEM((rows, 128), jnp.float32)],
        ),
        cost_estimate=pl.CostEstimate(
            flops=flops,
            transcendentals=rows * 3 * keys_rows * heads,
            bytes_accessed=2 * rows * width * 2 + 6 * keys_rows * width * 2,
        ),
    )(flags, q, *keys, *values)


def merge(o1, lse1, o2, lse2):
    rows, width = o1.shape
    heads = width // HEAD_DIM
    top = jnp.maximum(lse1, lse2)
    e1 = jnp.exp(lse1 - top)
    e2 = jnp.exp(lse2 - top)
    total = e1 + e2
    lse = top + jnp.log(total)
    w1 = jnp.transpose((e1 / total).reshape(heads, rows))[:, :, None]
    w2 = jnp.transpose((e2 / total).reshape(heads, rows))[:, :, None]
    o = o1.reshape(rows, heads, HEAD_DIM).astype(jnp.float32) * w1
    o = o + o2.reshape(rows, heads, HEAD_DIM).astype(jnp.float32) * w2
    return o.reshape(rows, width), lse


def shift_tm(x, by):
    size = lax.axis_size("tm")
    pairs = [(i, i + by) for i in range(size) if 0 <= i + by < size]
    return lax.ppermute(x, "tm", pairs)


def on_device(query_states, key_states, value_states, history, neighbours):
    _, rows, width = query_states.shape
    heads = width // HEAD_DIM
    seg = lax.axis_index("tm")
    tile = lax.axis_index("space")
    tiles = lax.axis_size("space")
    q = query_states[0]
    k = key_states[0]
    v = value_states[0]

    count = tiles
    from_left = [(i, i + 1) for i in range(count - 1)]
    from_right = [(i + 1, i) for i in range(count - 1)]
    k_l, v_l = lax.ppermute((k, v), "space", from_left)
    k_r, v_r = lax.ppermute((k, v), "space", from_right)
    keys = (k_l, k, k_r)
    values = (v_l, v, v_r)

    meta = jnp.concatenate([history.reshape(1), neighbours.reshape(2)]).astype(jnp.int32)
    tile_l = tile > 0
    tile_r = tile < tiles - 1

    def flags_for(m, d):
        seg_ok = m[0] >= d
        return jnp.stack(
            [
                ((m[1] == 1) & tile_l).astype(jnp.int32),
                seg_ok.astype(jnp.int32),
                ((m[2] == 1) & tile_r).astype(jnp.int32),
            ]
        )

    chunk_w = width // CHUNKS
    outs = []
    meta1 = None
    for c in range(CHUNKS):
        qc = q[:, c * chunk_w : (c + 1) * chunk_w]
        if c == 0:
            q1, meta1 = shift_tm((qc, meta), -1)
            q2, meta2 = shift_tm((q1, meta1), -1)
        else:
            q1 = shift_tm(qc, -1)
            q2 = shift_tm(q1, -1)
        f0 = flags_for(meta, 0)
        f1 = flags_for(meta1, 1)
        f2 = flags_for(meta2, 2)
        groups_c = chunk_w // HEAD_DIM // HG
        base = c * groups_c
        o0, l0 = attend(f0, q, keys, values, chunk_w, base, base)
        o1, l1 = attend(f1, q1, keys, values, chunk_w, base, 0)
        o2, l2 = attend(f2, q2, keys, values, chunk_w, base, 0)
        o2_in, l2_in = shift_tm((o2, l2), 1)
        l2_in = jnp.where(seg >= 1, l2_in, NEG)
        oc, lc = merge(o1, l1, o2_in, l2_in)
        oc_in, lc_in = shift_tm((oc.astype(jnp.bfloat16), lc), 1)
        lc_in = jnp.where(seg >= 1, lc_in, NEG)
        out, _ = merge(o0, l0, oc_in, lc_in)
        outs.append(out.astype(jnp.bfloat16))
    result = outs[0] if CHUNKS == 1 else jnp.concatenate(outs, axis=1)
    return result.reshape(1, rows, width)


def solution(mesh):
    placed = (
        P("tm", "space", None),
        P("tm", "space", None),
        P("tm", "space", None),
        P("tm"),
        P("tm", "space", None),
    )
    return jax.shard_map(
        on_device, mesh=mesh, in_specs=placed, out_specs=P("tm", "space", None), check_vma=False
    )
```

time: 454 us -> 183 us (0.40)
  the two profiles are of different devices: /device:TPU:112 before, /device:TPU:88 now
where the time goes in v1:
time: 183 us
  waiting for transfers between devices  78.5 us (43%)
  starting transfers between devices  36.7 us (20%)
  Pallas kernels  35.9 us (20%)
  other arithmetic  14.2 us (8%)
  local copies, waits for them, and re-layouts  11.2 us (6%)
  between operations  6 us (3%)
    ppermute x8, waiting for transfers between devices, shift_tm(): return lax.ppermute(x, 'tm', pairs)  72.5 us
    pallas_call x3, Pallas kernels, attend(): pl.pallas_call(_attn_kernel, out_shape=(jax.ShapeDtypeStruct((rows, width...  35.9 us
    ppermute x8, starting transfers between devices, shift_tm(): return lax.ppermute(x, 'tm', pairs)  27.3 us
    ppermute x2, waiting for transfers between devices, on_device(): k_r, v_r = lax.ppermute((k, v), 'space', from_right)  5.95 us
    ppermute x2, starting transfers between devices, on_device(): k_r, v_r = lax.ppermute((k, v), 'space', from_right)  5.56 us
    convert_element_type x1, other arithmetic, on_device(): oc_in, lc_in = shift_tm((oc.astype(jnp.bfloat16), lc), 1)  5.04 us
    reshape x1, other arithmetic, on_device(): return result.reshape(1, rows, width)  5.02 us
    mul x4, local copies, waits for them, and re-layouts, merge(): o = o1.reshape(rows, heads, HEAD_DIM).astype(jnp.float32) * w1  4.68 us
  transfers between devices with their start and end apart: 12, of which 6 were waited for; matrix products, arithmetic and copies ran while one was open for 8% of the time, Pallas kernels for 13%

profile of v1, /device:TPU:88, one launch (start us, length us, event | category | flops | bytes accessed | tf_op | source)
XLA Modules:
  0.0 182.6 jit_solution(8752487973064856973)
XLA Ops:
  0.0 4.2 %collective-permute-start.5 = (bf16[256,2560]{1,0:T(8,128)(2,1)}, bf16[256,2560]{1,0:T(8,128)(2,1)}, u32[]{:S(2)}, u32[]{:S(2)}) collective-permute-start(bf16[256,2560]{1,0:T(8,128)(2,1)} %bitcast.40), channel_id=1, source_target_pairs={{8,0},{16,8},{24,16},{32,24},{40,32},{48,40},{56,48},{64,56},{72,6... | collective-permute-start | bytes 3932168 | tf_op jit(solution)/shard_map/ppermute | solution.py:114
  4.2 1.9 %collective-permute-start = (bf16[256,2560]{1,0:T(8,128)(2,1)}, bf16[256,2560]{1,0:T(8,128)(2,1)S(1)}, u32[]{:S(2)}, u32[]{:S(2)}) collective-permute-start(bf16[256,2560]{1,0:T(8,128)(2,1)} %bitcast.26), channel_id=1, source_target_pairs={{0,1},{1,2},{2,3},{3,4},{4,5},{5,6},{6,7},{8,9},{9,10},{10,11},{11... | collective-permute-start | bytes 3932168 | tf_op jit(solution)/shard_map/ppermute | solution.py:130
  6.1 3.6 %collective-permute-start.1 = (bf16[256,2560]{1,0:T(8,128)(2,1)}, bf16[256,2560]{1,0:T(8,128)(2,1)S(1)}, u32[]{:S(2)}, u32[]{:S(2)}) collective-permute-start(bf16[256,2560]{1,0:T(8,128)(2,1)} %bitcast.27), channel_id=1, source_target_pairs={{1,0},{2,1},{3,2},{4,3},{5,4},{6,5},{7,6},{9,8},{10,9},{11,10},{12... | collective-permute-start | bytes 3932168 | tf_op jit(solution)/shard_map/ppermute | solution.py:131
  9.8 1.9 %collective-permute-start.2 = (bf16[256,2560]{1,0:T(8,128)(2,1)}, bf16[256,2560]{1,0:T(8,128)(2,1)}, u32[]{:S(2)}, u32[]{:S(2)}) collective-permute-start(bf16[256,2560]{1,0:T(8,128)(2,1)} %bitcast.31), channel_id=1, source_target_pairs={{0,1},{1,2},{2,3},{3,4},{4,5},{5,6},{6,7},{8,9},{9,10},{10,11},{11... | collective-permute-start | bytes 3932168 | tf_op jit(solution)/shard_map/ppermute | solution.py:130
  13.1 2.7 %collective-permute-start.4 = (s32[3]{0:T(128)S(1)}, s32[3]{0:T(128)S(1)}, u32[]{:S(2)}, u32[]{:S(2)}) collective-permute-start(s32[3]{0:T(128)S(1)} %pad_add_fusion), channel_id=1, source_target_pairs={{8,0},{16,8},{24,16},{32,24},{40,32},{48,40},{56,48},{64,56},{72,6... | collective-permute-start | bytes 44 | tf_op jit(solution)/shard_map/ppermute | solution.py:114
  15.8 16.9 %collective-permute-done.4 = s32[3]{0:T(128)S(1)} collective-permute-done((s32[3]{0:T(128)S(1)}, s32[3]{0:T(128)S(1)}, u32[]{:S(2)}, u32[]{:S(2)}) %collective-permute-start.4) | collective-permute-done | bytes 44 | tf_op jit(solution)/shard_map/ppermute | solution.py:114
  32.7 6.3 %collective-permute-start.6 = (s32[3]{0:T(128)S(1)}, s32[3]{0:T(128)S(1)}, u32[]{:S(2)}, u32[]{:S(2)}) collective-permute-start(s32[3]{0:T(128)S(1)} %collective-permute-done.4), channel_id=1, source_target_pairs={{8,0},{16,8},{24,16},{32,24},{40,32},{48,40},{56,48},{64,56},{72,6... | collective-permute-start | bytes 44 | tf_op jit(solution)/shard_map/ppermute | solution.py:114
  40.3 1.9 %collective-permute-start.3 = (bf16[256,2560]{1,0:T(8,128)(2,1)}, bf16[256,2560]{1,0:T(8,128)(2,1)}, u32[]{:S(2)}, u32[]{:S(2)}) collective-permute-start(bf16[256,2560]{1,0:T(8,128)(2,1)} %bitcast.32), channel_id=1, source_target_pairs={{1,0},{2,1},{3,2},{4,3},{5,4},{6,5},{7,6},{9,8},{10,9},{11,10},{12... | collective-permute-start | bytes 3932168 | tf_op jit(solution)/shard_map/ppermute | solution.py:131
  42.2 6.3 %collective-permute-start.7 = (bf16[256,2560]{1,0:T(8,128)(2,1)}, bf16[256,2560]{1,0:T(8,128)(2,1)}, u32[]{:S(2)}, u32[]{:S(2)}) collective-permute-start(bf16[256,2560]{1,0:T(8,128)(2,1)} %collective-permute-done.5.q_ref), channel_id=1, source_target_pairs={{8,0},{16,8},{24,16},{32,24},{40,32},{48,40},{56,48},{64,56},{72,6... | collective-permute-start | bytes 3932168 | tf_op jit(solution)/shard_map/ppermute | solution.py:114
  51.7 6.0 %collective-permute-done.3.vr_ref = bf16[256,2560]{1,0:T(8,128)(2,1)} collective-permute-done((bf16[256,2560]{1,0:T(8,128)(2,1)}, bf16[256,2560]{1,0:T(8,128)(2,1)}, u32[]{:S(2)}, u32[]{:S(2)}) %collective-permute-start.3) | collective-permute-done | bytes 1310752 | tf_op jit(solution)/shard_map/ppermute | solution.py:131
  57.7 19.8 %collective-permute-done.7.q_ref = bf16[256,2560]{1,0:T(8,128)(2,1)} collective-permute-done((bf16[256,2560]{1,0:T(8,128)(2,1)}, bf16[256,2560]{1,0:T(8,128)(2,1)}, u32[]{:S(2)}, u32[]{:S(2)}) %collective-permute-start.7) | collective-permute-done | bytes 1310752 | tf_op jit(solution)/shard_map/ppermute | solution.py:114
  77.5 12.0 %shard_map.57 = (bf16[256,2560]{1,0:T(8,128)(2,1)}, f32[4,5,256]{2,1,0:T(8,128)}) custom-call(s32[3]{0:T(128)} %add_convert_fusion.4.flags_ref, bf16[256,2560]{1,0:T(8,128)(2,1)} %collective-permute-done.7.q_ref, bf16[256,2560]{1,0:T(8,128)(2,1)} %copy-done, bf16[256,2560]{1,0:T(8,128)(2,1)} %bitcast.28, bf16[256,2560]{1,0:T(8,128)(2,1)} %copy-done.1, ...), custom_call_target="tpu_custom_call" | custom-call | flops 2013265920 | bytes 10485760 | tf_op jit(solution)/shard_map/pallas_call | solution.py:72
  89.5 1.9 %collective-permute-start.10 = (bf16[256,2560]{1,0:T(8,128)(2,1)}, bf16[256,2560]{1,0:T(8,128)(2,1)}, u32[]{:S(2)}, u32[]{:S(2)}) collective-permute-start(bf16[256,2560]{1,0:T(8,128)(2,1)} %get-tuple-element.16), channel_id=1, source_target_pairs={{0,8},{8,16},{16,24},{24,32},{32,40},{40,48},{48,56},{56,64},{64,7... | collective-permute-start | bytes 3932168 | tf_op jit(solution)/shard_map/ppermute | solution.py:114
  96.6 12.0 %shard_map.56 = (bf16[256,2560]{1,0:T(8,128)(2,1)}, f32[4,5,256]{2,1,0:T(8,128)}) custom-call(s32[3]{0:T(128)} %add_convert_fusion.3.flags_ref, bf16[256,2560]{1,0:T(8,128)(2,1)} %collective-permute-done.5.q_ref, bf16[256,2560]{1,0:T(8,128)(2,1)} %copy-done, bf16[256,2560]{1,0:T(8,128)(2,1)} %bitcast.29, bf16[256,2560]{1,0:T(8,128)(2,1)} %copy-done.1, ...), custom_call_target="tpu_custom_call" | custom-call | flops 2013265920 | bytes 10485760 | tf_op jit(solution)/shard_map/pallas_call | solution.py:72
  108.6 17.6 %collective-permute-done.8 = f32[4,5,256]{2,1,0:T(8,128)S(1)} collective-permute-done((f32[4,5,256]{2,1,0:T(8,128)}, f32[4,5,256]{2,1,0:T(8,128)S(1)}, u32[]{:S(2)}, u32[]{:S(2)}) %collective-permute-start.8) | collective-permute-done | bytes 20512 | tf_op jit(solution)/shard_map/ppermute | solution.py:114
  127.1 2.1 %copy.12 = f32[256,2560]{1,0:T(8,128)} copy(f32[256,2560]{0,1:T(8,128)S(1)} %bitcast.36) | data formatting | bytes 5242880 | tf_op jit(solution)/shard_map/mul | solution.py:107
  129.5 2.1 %copy.11 = f32[256,2560]{1,0:T(8,128)} copy(f32[256,2560]{0,1:T(8,128)S(1)} %bitcast.37) | data formatting | bytes 5242880 | tf_op jit(solution)/shard_map/mul | solution.py:106
  131.6 5.0 %add_convert_fusion.1 = bf16[256,2560]{1,0:T(8,128)(2,1)} fusion(f32[256,2560]{1,0:T(8,128)} %copy.12, bf16[256,2560]{1,0:T(8,128)(2,1)} %collective-permute-done.10, f32[256,2560]{1,0:T(8,128)} %copy.11, bf16[256,2560]{1,0:T(8,128)(2,1)} %get-tuple-element.15), kind=kLoop, calls=%fused_computation.1 | loop fusion | flops 3932160 | bytes 9175040 | tf_op jit(solution)/shard_map/convert_element_type | solution.py:171
  141.1 2.1 %collective-permute-start.9 = (f32[4,5,256]{2,1,0:T(8,128)S(1)}, f32[4,5,256]{2,1,0:T(8,128)S(1)}, u32[]{:S(2)}, u32[]{:S(2)}) collective-permute-start(f32[4,5,256]{2,1,0:T(8,128)S(1)} %get-tuple-element.20), channel_id=1, source_target_pairs={{0,8},{8,16},{16,24},{24,32},{32,40},{40,48},{48,56},{56,64},{64,7... | collective-permute-start | bytes 61448 | tf_op jit(solution)/shard_map/ppermute | solution.py:114
  143.2 12.0 %shard_map.55 = (bf16[256,2560]{1,0:T(8,128)(2,1)}, f32[4,5,256]{2,1,0:T(8,128)}) custom-call(s32[3]{0:T(128)} %add_convert_fusion.2.flags_ref, bf16[256,2560]{1,0:T(8,128)(2,1)} %bitcast.41, bf16[256,2560]{1,0:T(8,128)(2,1)} %copy-done, bf16[256,2560]{1,0:T(8,128)(2,1)} %bitcast.30, bf16[256,2560]{1,0:T(8,128)(2,1)} %copy-done.1, ...), custom_call_target="tpu_custom_call" | custom-call | flops 2013265920 | bytes 10485760 | tf_op jit(solution)/shard_map/pallas_call | solution.py:72
  155.1 16.9 %collective-permute-done.9 = f32[4,5,256]{2,1,0:T(8,128)S(1)} collective-permute-done((f32[4,5,256]{2,1,0:T(8,128)S(1)}, f32[4,5,256]{2,1,0:T(8,128)S(1)}, u32[]{:S(2)}, u32[]{:S(2)}) %collective-permute-start.9) | collective-permute-done | bytes 20512 | tf_op jit(solution)/shard_map/ppermute | solution.py:114
  173.1 2.1 %copy.13 = f32[256,2560]{1,0:T(8,128)} copy(f32[256,2560]{0,1:T(8,128)S(1)} %bitcast.38) | data formatting | bytes 5242880 | tf_op jit(solution)/shard_map/mul | solution.py:107
  175.4 2.1 %copy.10 = f32[256,2560]{1,0:T(8,128)} copy(f32[256,2560]{0,1:T(8,128)S(1)} %bitcast.39) | data formatting | bytes 5242880 | tf_op jit(solution)/shard_map/mul | solution.py:106
  177.5 5.0 %fusion = bf16[1,256,2560]{2,1,0:T(8,128)(2,1)} fusion(f32[256,2560]{1,0:T(8,128)} %copy.13, bf16[256,2560]{1,0:T(8,128)(2,1)} %collective-permute-done.11, f32[256,2560]{1,0:T(8,128)} %copy.10, bf16[256,2560]{1,0:T(8,128)(2,1)} %get-tuple-element.11), kind=kLoop, calls=%fused_computation.2 | loop fusion | flops 3932160 | bytes 9175040 | tf_op jit(solution)/shard_map/reshape | solution.py:176
  (32 shorter events, 12.0 us)
Async XLA Ops:
  0.0 42.2 %collective-permute-start.5 = (bf16[256,2560]{1,0:T(8,128)(2,1)}, bf16[256,2560]{1,0:T(8,128)(2,1)}, u32[]{:S(2)}, u32[]{:S(2)}) collective-permute-start(bf16[256,2560]{1,0:T(8,128)(2,1)} %bitcast.40), channel_id=1, source_target_pairs={{8,0},{16,8},{24,16},{32,24},{40,32},{48,40},{56,48},{64,56},{72,6... | collective-permute-start | bytes 3932168 | tf_op jit(solution)/shard_map/ppermute | solution.py:114
  4.2 47.5 %collective-permute-start = (bf16[256,2560]{1,0:T(8,128)(2,1)}, bf16[256,2560]{1,0:T(8,128)(2,1)S(1)}, u32[]{:S(2)}, u32[]{:S(2)}) collective-permute-start(bf16[256,2560]{1,0:T(8,128)(2,1)} %bitcast.26), channel_id=1, source_target_pairs={{0,1},{1,2},{2,3},{3,4},{4,5},{5,6},{6,7},{8,9},{9,10},{10,11},{11... | collective-permute-start | bytes 3932168 | tf_op jit(solution)/shard_map/ppermute | solution.py:130
  6.1 45.5 %collective-permute-start.1 = (bf16[256,2560]{1,0:T(8,128)(2,1)}, bf16[256,2560]{1,0:T(8,128)(2,1)S(1)}, u32[]{:S(2)}, u32[]{:S(2)}) collective-permute-start(bf16[256,2560]{1,0:T(8,128)(2,1)} %bitcast.27), channel_id=1, source_target_pairs={{1,0},{2,1},{3,2},{4,3},{5,4},{6,5},{7,6},{9,8},{10,9},{11,10},{12... | collective-permute-start | bytes 3932168 | tf_op jit(solution)/shard_map/ppermute | solution.py:131
  9.8 41.9 %collective-permute-start.2 = (bf16[256,2560]{1,0:T(8,128)(2,1)}, bf16[256,2560]{1,0:T(8,128)(2,1)}, u32[]{:S(2)}, u32[]{:S(2)}) collective-permute-start(bf16[256,2560]{1,0:T(8,128)(2,1)} %bitcast.31), channel_id=1, source_target_pairs={{0,1},{1,2},{2,3},{3,4},{4,5},{5,6},{6,7},{8,9},{9,10},{10,11},{11... | collective-permute-start | bytes 3932168 | tf_op jit(solution)/shard_map/ppermute | solution.py:130
  13.1 19.6 %collective-permute-start.4 = (s32[3]{0:T(128)S(1)}, s32[3]{0:T(128)S(1)}, u32[]{:S(2)}, u32[]{:S(2)}) collective-permute-start(s32[3]{0:T(128)S(1)} %pad_add_fusion), channel_id=1, source_target_pairs={{8,0},{16,8},{24,16},{32,24},{40,32},{48,40},{56,48},{64,56},{72,6... | collective-permute-start | bytes 44 | tf_op jit(solution)/shard_map/ppermute | solution.py:114
  32.7 7.6 %collective-permute-start.6 = (s32[3]{0:T(128)S(1)}, s32[3]{0:T(128)S(1)}, u32[]{:S(2)}, u32[]{:S(2)}) collective-permute-start(s32[3]{0:T(128)S(1)} %collective-permute-done.4), channel_id=1, source_target_pairs={{8,0},{16,8},{24,16},{32,24},{40,32},{48,40},{56,48},{64,56},{72,6... | collective-permute-start | bytes 44 | tf_op jit(solution)/shard_map/ppermute | solution.py:114
  40.3 17.3 %collective-permute-start.3 = (bf16[256,2560]{1,0:T(8,128)(2,1)}, bf16[256,2560]{1,0:T(8,128)(2,1)}, u32[]{:S(2)}, u32[]{:S(2)}) collective-permute-start(bf16[256,2560]{1,0:T(8,128)(2,1)} %bitcast.32), channel_id=1, source_target_pairs={{1,0},{2,1},{3,2},{4,3},{5,4},{6,5},{7,6},{9,8},{10,9},{11,10},{12... | collective-permute-start | bytes 3932168 | tf_op jit(solution)/shard_map/ppermute | solution.py:131
  42.2 35.2 %collective-permute-start.7 = (bf16[256,2560]{1,0:T(8,128)(2,1)}, bf16[256,2560]{1,0:T(8,128)(2,1)}, u32[]{:S(2)}, u32[]{:S(2)}) collective-permute-start(bf16[256,2560]{1,0:T(8,128)(2,1)} %collective-permute-done.5.q_ref), channel_id=1, source_target_pairs={{8,0},{16,8},{24,16},{32,24},{40,32},{48,40},{56,48},{64,56},{72,6... | collective-permute-start | bytes 3932168 | tf_op jit(solution)/shard_map/ppermute | solution.py:114
  51.7 25.8 %copy-start = (bf16[256,2560]{1,0:T(8,128)(2,1)}, bf16[256,2560]{1,0:T(8,128)(2,1)S(1)}, u32[]{:S(2)}) copy-start(bf16[256,2560]{1,0:T(8,128)(2,1)S(1)} %collective-permute-done.kl_ref) | copy-start | bytes 3932164
  51.7 25.8 %copy-start.1 = (bf16[256,2560]{1,0:T(8,128)(2,1)}, bf16[256,2560]{1,0:T(8,128)(2,1)S(1)}, u32[]{:S(2)}) copy-start(bf16[256,2560]{1,0:T(8,128)(2,1)S(1)} %collective-permute-done.1.kr_ref) | copy-start | bytes 3932164
  89.5 42.1 %collective-permute-start.10 = (bf16[256,2560]{1,0:T(8,128)(2,1)}, bf16[256,2560]{1,0:T(8,128)(2,1)}, u32[]{:S(2)}, u32[]{:S(2)}) collective-permute-start(bf16[256,2560]{1,0:T(8,128)(2,1)} %get-tuple-element.16), channel_id=1, source_target_pairs={{0,8},{8,16},{16,24},{24,32},{32,40},{40,48},{48,56},{56,64},{64,7... | collective-permute-start | bytes 3932168 | tf_op jit(solution)/shard_map/ppermute | solution.py:114
  94.7 31.5 %collective-permute-start.8 = (f32[4,5,256]{2,1,0:T(8,128)}, f32[4,5,256]{2,1,0:T(8,128)S(1)}, u32[]{:S(2)}, u32[]{:S(2)}) collective-permute-start(f32[4,5,256]{2,1,0:T(8,128)} %get-tuple-element.14), channel_id=1, source_target_pairs={{0,8},{8,16},{16,24},{24,32},{32,40},{40,48},{48,56},{56,64},{64,7... | collective-permute-start | bytes 61448 | tf_op jit(solution)/shard_map/ppermute | solution.py:114
  131.6 7.0 %copy-start.2 = (s32[1,1,2]{2,1,0:T(1,128)S(1)}, s32[1,1,2]{2,1,0:T(1,128)}, u32[]{:S(2)}) copy-start(s32[1,1,2]{2,1,0:T(1,128)} %param.9) | copy-start | bytes 28
  136.7 40.9 %collective-permute-start.11 = (bf16[256,2560]{1,0:T(8,128)(2,1)}, bf16[256,2560]{1,0:T(8,128)(2,1)}, u32[]{:S(2)}, u32[]{:S(2)}) collective-permute-start(bf16[256,2560]{1,0:T(8,128)(2,1)} %add_convert_fusion.1), channel_id=1, source_target_pairs={{0,8},{8,16},{16,24},{24,32},{32,40},{40,48},{48,56},{56,64},{64,7... | collective-permute-start | bytes 3932168 | tf_op jit(solution)/shard_map/ppermute | solution.py:114
  141.1 31.0 %collective-permute-start.9 = (f32[4,5,256]{2,1,0:T(8,128)S(1)}, f32[4,5,256]{2,1,0:T(8,128)S(1)}, u32[]{:S(2)}, u32[]{:S(2)}) collective-permute-start(f32[4,5,256]{2,1,0:T(8,128)S(1)} %get-tuple-element.20), channel_id=1, source_target_pairs={{0,8},{8,16},{16,24},{24,32},{32,40},{40,48},{48,56},{56,64},{64,7... | collective-permute-start | bytes 61448 | tf_op jit(solution)/shard_map/ppermute | solution.py:114

commit v2 on v1

v2 whole, which is shorter than its diff:
```python
import jax
import jax.numpy as jnp
from jax import lax
from jax.experimental import pallas as pl
from jax.experimental.pallas import tpu as pltpu
from jax.sharding import PartitionSpec as P

HEAD_DIM = 128
HG = 5
CHUNKS = 2
NEG = -1e30


def _attn_kernel(flags_ref, q_ref, kl_ref, kc_ref, kr_ref, vl_ref, vc_ref, vr_ref, o_ref, lse_ref, col_ref, m_ref, l_ref, acc_ref):
    hg = q_ref.shape[1] // HEAD_DIM
    inv_root = 1.0 / HEAD_DIM**0.5
    seg_ok = flags_ref[1] == 1

    @pl.when(seg_ok)
    def _():
        for h in range(hg):
            cols = slice(h * HEAD_DIM, (h + 1) * HEAD_DIM)
            q = q_ref[:, cols]

            def scores(k_ref):
                return (
                    lax.dot_general(
                        q, k_ref[:, cols], (((1,), (1,)), ((), ())), preferred_element_type=jnp.float32
                    )
                    * inv_root
                )

            s = scores(kc_ref)
            m = s.max(axis=1, keepdims=True)
            p = jnp.exp(s - m)
            m_ref[...] = m
            l_ref[...] = p.sum(axis=1, keepdims=True)
            acc_ref[...] = jnp.dot(p.astype(jnp.bfloat16), vc_ref[:, cols], preferred_element_type=jnp.float32)
            for flag_i, k_ref, v_ref in ((0, kl_ref, vl_ref), (2, kr_ref, vr_ref)):

                @pl.when(flags_ref[flag_i] == 1)
                def _():
                    s = scores(k_ref)
                    m_old = m_ref[...]
                    m_new = jnp.maximum(m_old, s.max(axis=1, keepdims=True))
                    alpha = jnp.exp(m_old - m_new)
                    p = jnp.exp(s - m_new)
                    l_ref[...] = alpha * l_ref[...] + p.sum(axis=1, keepdims=True)
                    acc_ref[...] = alpha * acc_ref[...] + jnp.dot(
                        p.astype(jnp.bfloat16), v_ref[:, cols], preferred_element_type=jnp.float32
                    )
                    m_ref[...] = m_new

            denom = l_ref[...]
            o_ref[:, cols] = (acc_ref[...] / denom).astype(o_ref.dtype)
            col_ref[:, h : h + 1] = m_ref[...] + jnp.log(denom)
        lse_ref[0] = jnp.transpose(col_ref[...])[:hg, :]

    @pl.when(jnp.logical_not(seg_ok))
    def _():
        o_ref[...] = jnp.zeros_like(o_ref)
        lse_ref[...] = jnp.full(lse_ref.shape, NEG, jnp.float32)


def attend(flags, q, keys, values, width, base, q_base):
    rows = q.shape[0]
    heads = width // HEAD_DIM
    groups = heads // HG
    lanes = HG * HEAD_DIM
    q_spec = pl.BlockSpec((rows, lanes), lambda g, f: (0, g + q_base))
    kv_spec = pl.BlockSpec((rows, lanes), lambda g, f: (0, g + base))
    keys_rows = keys[0].shape[0]
    return pl.pallas_call(
        _attn_kernel,
        out_shape=(
            jax.ShapeDtypeStruct((rows, width), jnp.bfloat16),
            jax.ShapeDtypeStruct((groups, HG, rows), jnp.float32),
        ),
        grid_spec=pltpu.PrefetchScalarGridSpec(
            num_scalar_prefetch=1,
            grid=(groups,),
            in_specs=[q_spec] + [kv_spec] * 6,
            out_specs=[
                pl.BlockSpec((rows, lanes), lambda g, f: (0, g)),
                pl.BlockSpec((1, HG, rows), lambda g, f: (g, 0, 0)),
            ],
            scratch_shapes=[
                pltpu.VMEM((rows, 128), jnp.float32),
                pltpu.VMEM((rows, 1), jnp.float32),
                pltpu.VMEM((rows, 1), jnp.float32),
                pltpu.VMEM((rows, HEAD_DIM), jnp.float32),
            ],
        ),
        cost_estimate=pl.CostEstimate(
            flops=4 * rows * 3 * keys_rows * HEAD_DIM * heads,
            transcendentals=rows * 3 * keys_rows * heads,
            bytes_accessed=2 * rows * width * 2 + 6 * keys_rows * width * 2,
        ),
    )(flags, q, *keys, *values)


def _merge_weights(valid_ref, l1_ref, l2_ref, wt_ref):
    hg = l1_ref.shape[1]
    l1 = l1_ref[0]
    l2 = jnp.where(valid_ref[0] == 1, l2_ref[0], NEG)
    top = jnp.maximum(l1, l2)
    e1 = jnp.exp(l1 - top)
    e2 = jnp.exp(l2 - top)
    total = e1 + e2
    wt_ref[0:hg, :] = e1 / total
    wt_ref[8 : 8 + hg, :] = e2 / total
    return top + jnp.log(total), jnp.transpose(wt_ref[...])


def _merge_body(o1_ref, o2_ref, o_ref, w, hg):
    for h in range(hg):
        cols = slice(h * HEAD_DIM, (h + 1) * HEAD_DIM)
        o = o1_ref[:, cols].astype(jnp.float32) * w[:, h : h + 1]
        o = o + o2_ref[:, cols].astype(jnp.float32) * w[:, 8 + h : 9 + h]
        o_ref[:, cols] = o.astype(o_ref.dtype)


def _merge_kernel(valid_ref, o1_ref, l1_ref, o2_ref, l2_ref, o_ref, l_ref, wt_ref):
    lse, w = _merge_weights(valid_ref, l1_ref, l2_ref, wt_ref)
    l_ref[0] = lse
    _merge_body(o1_ref, o2_ref, o_ref, w, l1_ref.shape[1])


def _final_kernel(valid_ref, o1_ref, l1_ref, o2_ref, l2_ref, o_ref, wt_ref):
    _, w = _merge_weights(valid_ref, l1_ref, l2_ref, wt_ref)
    _merge_body(o1_ref, o2_ref, o_ref, w, l1_ref.shape[1])


def merge(valid, o1, l1, o2, l2, base, final):
    rows, width = o2.shape
    groups = width // HEAD_DIM // HG
    lanes = HG * HEAD_DIM
    o1_spec = pl.BlockSpec((rows, lanes), lambda g, v: (0, g + base))
    l1_spec = pl.BlockSpec((1, HG, rows), lambda g, v: (g + base, 0, 0))
    o2_spec = pl.BlockSpec((rows, lanes), lambda g, v: (0, g))
    l2_spec = pl.BlockSpec((1, HG, rows), lambda g, v: (g, 0, 0))
    if final:
        kernel = _final_kernel
        out_shape = jax.ShapeDtypeStruct(o1.shape, o1.dtype)
        out_specs = o1_spec
        aliases = {1: 0}
    else:
        kernel = _merge_kernel
        out_shape = (
            jax.ShapeDtypeStruct((rows, width), jnp.bfloat16),
            jax.ShapeDtypeStruct((groups, HG, rows), jnp.float32),
        )
        out_specs = [o2_spec, l2_spec]
        aliases = {}
    return pl.pallas_call(
        kernel,
        out_shape=out_shape,
        grid_spec=pltpu.PrefetchScalarGridSpec(
            num_scalar_prefetch=1,
            grid=(groups,),
            in_specs=[o1_spec, l1_spec, o2_spec, l2_spec],
            out_specs=out_specs,
            scratch_shapes=[pltpu.VMEM((128, rows), jnp.float32)],
        ),
        input_output_aliases=aliases,
        cost_estimate=pl.CostEstimate(
            flops=4 * rows * width, transcendentals=0, bytes_accessed=3 * rows * width * 2
        ),
    )(valid, o1, l1, o2, l2)


def shift_tm(x, by):
    size = lax.axis_size("tm")
    pairs = [(i, i + by) for i in range(size) if 0 <= i + by < size]
    return lax.ppermute(x, "tm", pairs)


def on_device(query_states, key_states, value_states, history, neighbours):
    _, rows, width = query_states.shape
    seg = lax.axis_index("tm")
    tile = lax.axis_index("space")
    tiles = lax.axis_size("space")
    q = query_states[0]
    k = key_states[0]
    v = value_states[0]

    meta = jnp.concatenate([history.reshape(1), neighbours.reshape(2)]).astype(jnp.int32)
    meta1 = shift_tm(meta, -1)
    meta2 = shift_tm(meta, -2)

    from_left = [(i, i + 1) for i in range(tiles - 1)]
    from_right = [(i + 1, i) for i in range(tiles - 1)]
    k_l, v_l = lax.ppermute((k, v), "space", from_left)
    k_r, v_r = lax.ppermute((k, v), "space", from_right)
    keys = (k_l, k, k_r)
    values = (v_l, v, v_r)

    tile_l = tile > 0
    tile_r = tile < tiles - 1

    def flags_for(m, d):
        return jnp.stack(
            [
                ((m[1] == 1) & tile_l).astype(jnp.int32),
                (m[0] >= d).astype(jnp.int32),
                ((m[2] == 1) & tile_r).astype(jnp.int32),
            ]
        )

    valid = (seg >= 1).astype(jnp.int32).reshape(1)
    chunk_w = width // CHUNKS
    groups_c = chunk_w // HEAD_DIM // HG
    q1s, q2s = [], []
    for c in range(CHUNKS):
        q1s.append(shift_tm(q[:, c * chunk_w : (c + 1) * chunk_w], -1))
    for c in range(CHUNKS):
        q2s.append(shift_tm(q1s[c], -1))
    o_self, l_self = attend(flags_for(meta, 0), q, keys, values, width, 0, 0)
    f1 = flags_for(meta1, 1)
    f2 = flags_for(meta2, 2)
    result = o_self
    for c in range(CHUNKS):
        base = c * groups_c
        o1, l1 = attend(f1, q1s[c], keys, values, chunk_w, base, 0)
        o2, l2 = attend(f2, q2s[c], keys, values, chunk_w, base, 0)
        o2_in, l2_in = shift_tm((o2, l2), 1)
        oc, lc = merge(valid, o1, l1, o2_in, l2_in, 0, False)
        oc_in, lc_in = shift_tm((oc, lc), 1)
        result = merge(valid, result, l_self, oc_in, lc_in, base, True)
    return result.reshape(1, rows, width)


def solution(mesh):
    placed = (
        P("tm", "space", None),
        P("tm", "space", None),
        P("tm", "space", None),
        P("tm"),
        P("tm", "space", None),
    )
    return jax.shard_map(
        on_device, mesh=mesh, in_specs=placed, out_specs=P("tm", "space", None), check_vma=False
    )
```

time: 183 us -> 225 us (1.23)
  the two profiles are of different devices: /device:TPU:88 before, /device:TPU:16 now
where the time goes in v2:
time: 225 us
  Pallas kernels  91.1 us (40%)
  starting transfers between devices  74 us (33%)
  waiting for transfers between devices  43.1 us (19%)
  local copies, waits for them, and re-layouts  8.48 us (4%)
  between operations  6.04 us (3%)
    pallas_call x5, Pallas kernels, attend(): pl.pallas_call(_attn_kernel, out_shape=(jax.ShapeDtypeStruct((rows, width...  79.4 us
    ppermute x14, starting transfers between devices, shift_tm(): return lax.ppermute(x, 'tm', pairs)  64.6 us
    ppermute x14, waiting for transfers between devices, shift_tm(): return lax.ppermute(x, 'tm', pairs)  43.1 us
    pallas_call x4, Pallas kernels, merge(): pl.pallas_call(kernel, out_shape=out_shape, grid_spec=pltpu.PrefetchScala...  11.8 us
    ppermute x2, starting transfers between devices, on_device(): k_r, v_r = lax.ppermute((k, v), 'space', from_right)  5.55 us
    unnamed x30, local copies, waits for them, and re-layouts  5.01 us
  transfers between devices with their start and end apart: 18, of which 5 were waited for; matrix products, arithmetic and copies ran while one was open for 2% of the time, Pallas kernels for 39%

profile of v2, /device:TPU:16, one launch (start us, length us, event | category | flops | bytes accessed | tf_op | source)
XLA Modules:
  0.0 224.7 jit_solution(3862599818727437485)
XLA Ops:
  0.0 1.5 fusion
  2.8 1.9 collective-permute-start
  4.8 3.6 %collective-permute-start.1 = (bf16[256,2560]{1,0:T(8,128)(2,1)S(1)}, bf16[256,2560]{1,0:T(8,128)(2,1)}, u32[]{:S(2)}, u32[]{:S(2)}) collective-permute-start(bf16[256,2560]{1,0:T(8,128)(2,1)S(1)} %bitcast.24), channel_id=1, source_target_pairs={{1,0},{2,1},{3,2},{4,3},{5,4},{6,5},{7,6},{9,8},{10,9},{11,10},{12... | collective-permute-start | bytes 3932168 | tf_op jit(solution)/shard_map/ppermute | solution.py:194
  10.5 1.9 collective-permute-start.2
  12.4 4.4 %collective-permute-done.6 = s32[3]{0:T(128)S(1)} collective-permute-done((s32[3]{0:T(128)S(1)}, s32[3]{0:T(128)S(1)}, u32[]{:S(2)}, u32[]{:S(2)}) %collective-permute-start.6) | collective-permute-done | bytes 44 | tf_op jit(solution)/shard_map/ppermute | solution.py:175
  16.7 1.9 collective-permute-start.3
  21.2 20.5 %collective-permute-done.5.q_ref = bf16[256,1280]{1,0:T(8,128)(2,1)} collective-permute-done((bf16[256,1280]{1,0:T(8,128)(2,1)S(1)}, bf16[256,1280]{1,0:T(8,128)(2,1)}, u32[]{:S(2)}, u32[]{:S(2)}) %collective-permute-start.5) | collective-permute-done | bytes 655392 | tf_op jit(solution)/shard_map/ppermute | solution.py:175
  48.6 12.9 %collective-permute-done.7.q_ref = bf16[256,1280]{1,0:T(8,128)(2,1)} collective-permute-done((bf16[256,1280]{1,0:T(8,128)(2,1)}, bf16[256,1280]{1,0:T(8,128)(2,1)}, u32[]{:S(2)}, u32[]{:S(2)}) %collective-permute-start.7) | collective-permute-done | bytes 655392 | tf_op jit(solution)/shard_map/ppermute | solution.py:175
  61.5 18.7 %shard_map.57 = (bf16[256,1280]{1,0:T(8,128)(2,1)}, f32[2,5,256]{2,1,0:T(8,128)}) custom-call(s32[3]{0:T(128)} %add_convert_fusion.2.flags_ref, bf16[256,1280]{1,0:T(8,128)(2,1)} %collective-permute-done.7.q_ref, bf16[256,2560]{1,0:T(8,128)(2,1)} %copy-done.2, bf16[256,2560]{1,0:T(8,128)(2,1)} %bitcast.18, bf16[256,2560]{1,0:T(8,128)(2,1)} %collective-permute-done.1.kr_ref, ...), custom_call_target="tpu_custom_call" | custom-call | flops 1006632960 | bytes 5242880 | tf_op jit(solution)/shard_map/pallas_call | solution.py:73
  81.5 18.8 %shard_map.61 = (bf16[256,1280]{1,0:T(8,128)(2,1)}, f32[2,5,256]{2,1,0:T(8,128)}) custom-call(s32[3]{0:T(128)} %add_convert_fusion.2.flags_ref, bf16[256,1280]{1,0:T(8,128)(2,1)} %collective-permute-done.13.q_ref, bf16[256,2560]{1,0:T(8,128)(2,1)} %copy-done.2, bf16[256,2560]{1,0:T(8,128)(2,1)} %bitcast.19, bf16[256,2560]{1,0:T(8,128)(2,1)} %collective-permute-done.1.kr_ref, ...), custom_call_target="tpu_custom_call" | custom-call | flops 1006632960 | bytes 5242880 | tf_op jit(solution)/shard_map/pallas_call | solution.py:73
  102.9 4.1 %collective-permute-done.4 = s32[3]{0:T(128)S(1)} collective-permute-done((s32[3]{0:T(128)S(1)}, s32[3]{0:T(128)S(1)}, u32[]{:S(2)}, u32[]{:S(2)}) %collective-permute-start.4) | collective-permute-done | bytes 44 | tf_op jit(solution)/shard_map/ppermute | solution.py:175
  110.1 10.1 %collective-permute-start.15 = (f32[2,5,256]{2,1,0:T(8,128)}, f32[2,5,256]{2,1,0:T(8,128)S(1)}, u32[]{:S(2)}, u32[]{:S(2)}) collective-permute-start(f32[2,5,256]{2,1,0:T(8,128)} %get-tuple-element.30), channel_id=1, source_target_pairs={{0,8},{8,16},{16,24},{24,32},{32,40},{40,48},{48,56},{56,64},{64,7... | collective-permute-start | bytes 30728 | tf_op jit(solution)/shard_map/ppermute | solution.py:175
  120.2 4.1 %collective-permute-start.9 = (f32[2,5,256]{2,1,0:T(8,128)S(1)}, f32[2,5,256]{2,1,0:T(8,128)S(1)}, u32[]{:S(2)}, u32[]{:S(2)}) collective-permute-start(f32[2,5,256]{2,1,0:T(8,128)S(1)} %copy-done.13), channel_id=1, source_target_pairs={{0,8},{8,16},{16,24},{24,32},{32,40},{40,48},{48,56},{56,64},{64,7... | collective-permute-start | bytes 30728 | tf_op jit(solution)/shard_map/ppermute | solution.py:175
  124.3 3.8 %shard_map.60 = (bf16[256,1280]{1,0:T(8,128)(2,1)}, f32[2,5,256]{2,1,0:T(8,128)}) custom-call(s32[3]{0:T(128)} %add_convert_fusion.1.flags_ref, bf16[256,1280]{1,0:T(8,128)(2,1)} %copy-done.3, bf16[256,2560]{1,0:T(8,128)(2,1)} %copy-done.2, bf16[256,2560]{1,0:T(8,128)(2,1)} %bitcast.20, bf16[256,2560]{1,0:T(8,128)(2,1)} %collective-permute-done.1.kr_ref, ...), custom_call_target="tpu_custom_call" | custom-call | flops 1006632960 | bytes 5242880 | tf_op jit(solution)/shard_map/pallas_call | solution.py:73
  128.1 3.7 %shard_map.56 = (bf16[256,1280]{1,0:T(8,128)(2,1)}, f32[2,5,256]{2,1,0:T(8,128)}) custom-call(s32[3]{0:T(128)} %add_convert_fusion.1.flags_ref, bf16[256,1280]{1,0:T(8,128)(2,1)} %collective-permute-done.5.q_ref, bf16[256,2560]{1,0:T(8,128)(2,1)} %copy-done.2, bf16[256,2560]{1,0:T(8,128)(2,1)} %bitcast.21, bf16[256,2560]{1,0:T(8,128)(2,1)} %collective-permute-done.1.kr_ref, ...), custom_call_target="tpu_custom_call" | custom-call | flops 1006632960 | bytes 5242880 | tf_op jit(solution)/shard_map/pallas_call | solution.py:73
  132.7 2.9 %shard_map.58 = (bf16[256,1280]{1,0:T(8,128)(2,1)}, f32[2,5,256]{2,1,0:T(8,128)}) custom-call(s32[1]{0:T(128)} %bitcast.valid_ref, bf16[256,1280]{1,0:T(8,128)(2,1)} %get-tuple-element.21.o1_ref, f32[2,5,256]{2,1,0:T(8,128)} %get-tuple-element.22.l1_ref, bf16[256,1280]{1,0:T(8,128)(2,1)} %copy-done.5, f32[2,5,256]{2,1,0:T(8,128)} %copy-done.10), custom_call_target="tpu_custom_call" | custom-call | flops 1310720 | bytes 1966080 | tf_op jit(solution)/shard_map/pallas_call | solution.py:155
  135.6 34.1 %collective-permute-start.10 = (bf16[256,1280]{1,0:T(8,128)(2,1)}, bf16[256,1280]{1,0:T(8,128)(2,1)S(1)}, u32[]{:S(2)}, u32[]{:S(2)}) collective-permute-start(bf16[256,1280]{1,0:T(8,128)(2,1)} %get-tuple-element.25), channel_id=1, source_target_pairs={{0,8},{8,16},{16,24},{24,32},{32,40},{40,48},{48,56},{56,64},{64,7... | collective-permute-start | bytes 1966088 | tf_op jit(solution)/shard_map/ppermute | solution.py:175
  170.6 3.0 %shard_map.62 = (bf16[256,1280]{1,0:T(8,128)(2,1)}, f32[2,5,256]{2,1,0:T(8,128)}) custom-call(s32[1]{0:T(128)} %bitcast.valid_ref, bf16[256,1280]{1,0:T(8,128)(2,1)} %get-tuple-element.27.o1_ref, f32[2,5,256]{2,1,0:T(8,128)} %get-tuple-element.28.l1_ref, bf16[256,1280]{1,0:T(8,128)(2,1)} %copy-done.4, f32[2,5,256]{2,1,0:T(8,128)} %copy-done.8), custom_call_target="tpu_custom_call" | custom-call | flops 1310720 | bytes 1966080 | tf_op jit(solution)/shard_map/pallas_call | solution.py:155
  173.6 1.9 collective-permute-start.16
  178.1 1.9 collective-permute-start.17
  180.0 2.1 collective-permute-start.11
  182.1 34.4 %shard_map.55 = (bf16[256,2560]{1,0:T(8,128)(2,1)}, f32[4,5,256]{2,1,0:T(8,128)}) custom-call(s32[3]{0:T(128)} %add_convert_fusion.flags_ref, bf16[256,2560]{1,0:T(8,128)(2,1)} %bitcast.33, bf16[256,2560]{1,0:T(8,128)(2,1)} %copy-done.2, bf16[256,2560]{1,0:T(8,128)(2,1)} %bitcast.22, bf16[256,2560]{1,0:T(8,128)(2,1)} %collective-permute-done.1.kr_ref, ...), custom_call_target="tpu_custom_call" | custom-call | flops 2013265920 | bytes 10485760 | tf_op jit(solution)/shard_map/pallas_call | solution.py:73
  217.4 2.9 %shard_map.59.o1_ref = bf16[256,2560]{1,0:T(8,128)(2,1)} custom-call(s32[1]{0:T(128)} %bitcast.valid_ref, bf16[256,2560]{1,0:T(8,128)(2,1)} %get-tuple-element.19.o1_ref, f32[4,5,256]{2,1,0:T(8,128)} %get-tuple-element.20.l1_ref, bf16[256,1280]{1,0:T(8,128)(2,1)} %copy-done.6, f32[2,5,256]{2,1,0:T(8,128)} %copy-done.11), custom_call_target="tpu_custom_call", output_to_operand_aliasing={{}: (1, {})} | custom-call | flops 1310720 | bytes 1966080 | tf_op jit(solution)/shard_map/pallas_call | solution.py:155
  221.8 2.9 %shard_map.63 = bf16[256,2560]{1,0:T(8,128)(2,1)} custom-call(s32[1]{0:T(128)} %bitcast.valid_ref, bf16[256,2560]{1,0:T(8,128)(2,1)} %shard_map.59.o1_ref, f32[4,5,256]{2,1,0:T(8,128)} %get-tuple-element.20.l1_ref, bf16[256,1280]{1,0:T(8,128)(2,1)} %copy-done.7, f32[2,5,256]{2,1,0:T(8,128)} %copy-done.9), custom_call_target="tpu_custom_call", output_to_operand_aliasing={{}: (1, {})} | custom-call | flops 1310720 | bytes 1966080 | tf_op jit(solution)/shard_map/pallas_call | solution.py:155
  (59 shorter events, 20.6 us)
Async XLA Ops:
  0.0 2.8 %copy-start = (bf16[1,256,2560]{2,1,0:T(8,128)(2,1)S(1)}, bf16[1,256,2560]{2,1,0:T(8,128)(2,1)}, u32[]{:S(2)}) copy-start(bf16[1,256,2560]{2,1,0:T(8,128)(2,1)} %param.6) | copy-start | bytes 3932164
  0.0 9.1 %copy-start.12 = (s32[1,1,2]{2,1,0:T(1,128)S(1)}, s32[1,1,2]{2,1,0:T(1,128)}, u32[]{:S(2)}) copy-start(s32[1,1,2]{2,1,0:T(1,128)} %param.9) | copy-start | bytes 28
  0.0 10.4 %copy-start.1 = (bf16[1,256,2560]{2,1,0:T(8,128)(2,1)S(1)}, bf16[1,256,2560]{2,1,0:T(8,128)(2,1)}, u32[]{:S(2)}) copy-start(bf16[1,256,2560]{2,1,0:T(8,128)(2,1)} %param.7) | copy-start | bytes 3932164
  1.5 18.4 %collective-permute-start.12 = (bf16[256,1280]{1,0:T(8,128)(2,1)S(1)}, bf16[256,1280]{1,0:T(8,128)(2,1)S(1)}, u32[]{:S(2)}, u32[]{:S(2)}) collective-permute-start(bf16[256,1280]{1,0:T(8,128)(2,1)S(1)} %get-tuple-element.33), channel_id=1, source_target_pairs={{8,0},{16,8},{24,16},{32,24},{40,32},{48,40},{56,48},{64,56},{72,6... | collective-permute-start | bytes 1966088 | tf_op jit(solution)/shard_map/ppermute | solution.py:175
  2.8 40.1 %collective-permute-start = (bf16[256,2560]{1,0:T(8,128)(2,1)S(1)}, bf16[256,2560]{1,0:T(8,128)(2,1)S(1)}, u32[]{:S(2)}, u32[]{:S(2)}) collective-permute-start(bf16[256,2560]{1,0:T(8,128)(2,1)S(1)} %bitcast.23), channel_id=1, source_target_pairs={{0,1},{1,2},{2,3},{3,4},{4,5},{5,6},{6,7},{8,9},{9,10},{10,11},{11... | collective-permute-start | bytes 3932168 | tf_op jit(solution)/shard_map/ppermute | solution.py:193
  4.8 43.8 %collective-permute-start.1 = (bf16[256,2560]{1,0:T(8,128)(2,1)S(1)}, bf16[256,2560]{1,0:T(8,128)(2,1)}, u32[]{:S(2)}, u32[]{:S(2)}) collective-permute-start(bf16[256,2560]{1,0:T(8,128)(2,1)S(1)} %bitcast.24), channel_id=1, source_target_pairs={{1,0},{2,1},{3,2},{4,3},{5,4},{6,5},{7,6},{9,8},{10,9},{11,10},{12... | collective-permute-start | bytes 3932168 | tf_op jit(solution)/shard_map/ppermute | solution.py:194
  9.2 7.6 %collective-permute-start.6 = (s32[3]{0:T(128)S(1)}, s32[3]{0:T(128)S(1)}, u32[]{:S(2)}, u32[]{:S(2)}) collective-permute-start(s32[3]{0:T(128)S(1)} %pad_add_fusion), channel_id=1, source_target_pairs={{16,0},{24,8},{32,16},{40,24},{48,32},{56,40},{64,48},{72,56},{80,... | collective-permute-start | bytes 44 | tf_op jit(solution)/shard_map/ppermute | solution.py:175
  10.5 38.1 %collective-permute-start.2 = (bf16[256,2560]{1,0:T(8,128)(2,1)S(1)}, bf16[256,2560]{1,0:T(8,128)(2,1)}, u32[]{:S(2)}, u32[]{:S(2)}) collective-permute-start(bf16[256,2560]{1,0:T(8,128)(2,1)S(1)} %bitcast.30), channel_id=1, source_target_pairs={{0,1},{1,2},{2,3},{3,4},{4,5},{5,6},{6,7},{8,9},{9,10},{10,11},{11... | collective-permute-start | bytes 3932168 | tf_op jit(solution)/shard_map/ppermute | solution.py:193
  16.7 31.8 %collective-permute-start.3 = (bf16[256,2560]{1,0:T(8,128)(2,1)S(1)}, bf16[256,2560]{1,0:T(8,128)(2,1)}, u32[]{:S(2)}, u32[]{:S(2)}) collective-permute-start(bf16[256,2560]{1,0:T(8,128)(2,1)S(1)} %bitcast.31), channel_id=1, source_target_pairs={{1,0},{2,1},{3,2},{4,3},{5,4},{6,5},{7,6},{9,8},{10,9},{11,10},{12... | collective-permute-start | bytes 3932168 | tf_op jit(solution)/shard_map/ppermute | solution.py:194
  19.9 60.3 %copy-start.3 = (bf16[256,1280]{1,0:T(8,128)(2,1)}, bf16[256,1280]{1,0:T(8,128)(2,1)S(1)}, u32[]{:S(2)}) copy-start(bf16[256,1280]{1,0:T(8,128)(2,1)S(1)} %collective-permute-done.12.q_ref) | copy-start | bytes 1966084
  19.9 21.7 %collective-permute-start.5 = (bf16[256,1280]{1,0:T(8,128)(2,1)S(1)}, bf16[256,1280]{1,0:T(8,128)(2,1)}, u32[]{:S(2)}, u32[]{:S(2)}) collective-permute-start(bf16[256,1280]{1,0:T(8,128)(2,1)S(1)} %get-tuple-element.34), channel_id=1, source_target_pairs={{8,0},{16,8},{24,16},{32,24},{40,32},{48,40},{56,48},{64,56},{72,6... | collective-permute-start | bytes 1966088 | tf_op jit(solution)/shard_map/ppermute | solution.py:175
  41.6 19.8 %collective-permute-start.7 = (bf16[256,1280]{1,0:T(8,128)(2,1)}, bf16[256,1280]{1,0:T(8,128)(2,1)}, u32[]{:S(2)}, u32[]{:S(2)}) collective-permute-start(bf16[256,1280]{1,0:T(8,128)(2,1)} %collective-permute-done.5.q_ref), channel_id=1, source_target_pairs={{8,0},{16,8},{24,16},{32,24},{40,32},{48,40},{56,48},{64,56},{72,6... | collective-permute-start | bytes 1966088 | tf_op jit(solution)/shard_map/ppermute | solution.py:175
  44.0 37.5 %collective-permute-start.13 = (bf16[256,1280]{1,0:T(8,128)(2,1)S(1)}, bf16[256,1280]{1,0:T(8,128)(2,1)}, u32[]{:S(2)}, u32[]{:S(2)}) collective-permute-start(bf16[256,1280]{1,0:T(8,128)(2,1)S(1)} %collective-permute-done.12.q_ref), channel_id=1, source_target_pairs={{8,0},{16,8},{24,16},{32,24},{40,32},{48,40},{56,48},{64,56},{72,6... | collective-permute-start | bytes 1966088 | tf_op jit(solution)/shard_map/ppermute | solution.py:175
  80.2 40.0 %copy-start.13 = (f32[2,5,256]{2,1,0:T(8,128)S(1)}, f32[2,5,256]{2,1,0:T(8,128)}, u32[]{:S(2)}) copy-start(f32[2,5,256]{2,1,0:T(8,128)} %get-tuple-element.24) | copy-start | bytes 30724
  80.2 51.6 %collective-permute-start.8 = (bf16[256,1280]{1,0:T(8,128)(2,1)}, bf16[256,1280]{1,0:T(8,128)(2,1)S(1)}, u32[]{:S(2)}, u32[]{:S(2)}) collective-permute-start(bf16[256,1280]{1,0:T(8,128)(2,1)} %get-tuple-element.23), channel_id=1, source_target_pairs={{0,8},{8,16},{16,24},{24,32},{32,40},{40,48},{48,56},{56,64},{64,7... | collective-permute-start | bytes 1966088 | tf_op jit(solution)/shard_map/ppermute | solution.py:175
  100.3 69.4 %collective-permute-start.14 = (bf16[256,1280]{1,0:T(8,128)(2,1)}, bf16[256,1280]{1,0:T(8,128)(2,1)S(1)}, u32[]{:S(2)}, u32[]{:S(2)}) collective-permute-start(bf16[256,1280]{1,0:T(8,128)(2,1)} %get-tuple-element.29), channel_id=1, source_target_pairs={{0,8},{8,16},{16,24},{24,32},{32,40},{40,48},{48,56},{56,64},{64,7... | collective-permute-start | bytes 1966088 | tf_op jit(solution)/shard_map/ppermute | solution.py:175
  101.6 5.4 %collective-permute-start.4 = (s32[3]{0:T(128)S(1)}, s32[3]{0:T(128)S(1)}, u32[]{:S(2)}, u32[]{:S(2)}) collective-permute-start(s32[3]{0:T(128)S(1)} %pad_add_fusion), channel_id=1, source_target_pairs={{8,0},{16,8},{24,16},{32,24},{40,32},{48,40},{56,48},{64,56},{72,6... | collective-permute-start | bytes 44 | tf_op jit(solution)/shard_map/ppermute | solution.py:175
  110.1 59.6 %collective-permute-start.15 = (f32[2,5,256]{2,1,0:T(8,128)}, f32[2,5,256]{2,1,0:T(8,128)S(1)}, u32[]{:S(2)}, u32[]{:S(2)}) collective-permute-start(f32[2,5,256]{2,1,0:T(8,128)} %get-tuple-element.30), channel_id=1, source_target_pairs={{0,8},{8,16},{16,24},{24,32},{32,40},{40,48},{48,56},{56,64},{64,7... | collective-permute-start | bytes 30728 | tf_op jit(solution)/shard_map/ppermute | solution.py:175
  120.2 11.6 %collective-permute-start.9 = (f32[2,5,256]{2,1,0:T(8,128)S(1)}, f32[2,5,256]{2,1,0:T(8,128)S(1)}, u32[]{:S(2)}, u32[]{:S(2)}) collective-permute-start(f32[2,5,256]{2,1,0:T(8,128)S(1)} %copy-done.13), channel_id=1, source_target_pairs={{0,8},{8,16},{16,24},{24,32},{32,40},{40,48},{48,56},{56,64},{64,7... | collective-permute-start | bytes 30728 | tf_op jit(solution)/shard_map/ppermute | solution.py:175
  135.6 44.4 %copy-start.14 = (f32[2,5,256]{2,1,0:T(8,128)S(1)}, f32[2,5,256]{2,1,0:T(8,128)}, u32[]{:S(2)}) copy-start(f32[2,5,256]{2,1,0:T(8,128)} %get-tuple-element.26) | copy-start | bytes 30724
  135.6 81.0 %collective-permute-start.10 = (bf16[256,1280]{1,0:T(8,128)(2,1)}, bf16[256,1280]{1,0:T(8,128)(2,1)S(1)}, u32[]{:S(2)}, u32[]{:S(2)}) collective-permute-start(bf16[256,1280]{1,0:T(8,128)(2,1)} %get-tuple-element.25), channel_id=1, source_target_pairs={{0,8},{8,16},{16,24},{24,32},{32,40},{40,48},{48,56},{56,64},{64,7... | collective-permute-start | bytes 1966088 | tf_op jit(solution)/shard_map/ppermute | solution.py:175
  173.6 46.8 %collective-permute-start.16 = (bf16[256,1280]{1,0:T(8,128)(2,1)}, bf16[256,1280]{1,0:T(8,128)(2,1)S(1)}, u32[]{:S(2)}, u32[]{:S(2)}) collective-permute-start(bf16[256,1280]{1,0:T(8,128)(2,1)} %get-tuple-element.31), channel_id=1, source_target_pairs={{0,8},{8,16},{16,24},{24,32},{32,40},{40,48},{48,56},{56,64},{64,7... | collective-permute-start | bytes 1966088 | tf_op jit(solution)/shard_map/ppermute | solution.py:175
  178.1 42.3 %collective-permute-start.17 = (f32[2,5,256]{2,1,0:T(8,128)}, f32[2,5,256]{2,1,0:T(8,128)S(1)}, u32[]{:S(2)}, u32[]{:S(2)}) collective-permute-start(f32[2,5,256]{2,1,0:T(8,128)} %get-tuple-element.32), channel_id=1, source_target_pairs={{0,8},{8,16},{16,24},{24,32},{32,40},{40,48},{48,56},{56,64},{64,7... | collective-permute-start | bytes 30728 | tf_op jit(solution)/shard_map/ppermute | solution.py:175
  180.0 36.6 %collective-permute-start.11 = (f32[2,5,256]{2,1,0:T(8,128)S(1)}, f32[2,5,256]{2,1,0:T(8,128)S(1)}, u32[]{:S(2)}, u32[]{:S(2)}) collective-permute-start(f32[2,5,256]{2,1,0:T(8,128)S(1)} %copy-done.14), channel_id=1, source_target_pairs={{0,8},{8,16},{16,24},{24,32},{32,40},{40,48},{48,56},{56,64},{64,7... | collective-permute-start | bytes 30728 | tf_op jit(solution)/shard_map/ppermute | solution.py:175
  (9 other events, 6.8 us)
